TPU v7x, 128 devices: a whole 4x4x4 slice. The times are simulated.
128 devices in a mesh: shot: 16 (over z, x_lo, core), brick: 8 (over y, x_hi).
Axes of the slice: x: 4 (x_hi: 2, x_lo: 2; x = x_hi * 2 + x_lo), y: 4, z: 4, core: 2. Of those that a mesh axis runs over, the one named last changes fastest.
Arguments:
- sources: float32 [16, 2, 2, 256, 64, 256], P('shot', None, None, None, 'brick'), may hold values from -24 to 24
- slowness: float32 [16, 256, 64, 256], P('shot', None, 'brick'), may hold values from 0.5 to 2
- group_size: int32 [16], replicated, may hold values from 2 to 8, as said below
- window_anchor: int32 [16], replicated, may hold values from 0 to 56
- tile_slot: int32 [64], replicated, may hold values from 0 to 63, each once
Outputs:
- gradient: float32 [8, 64, 65536], P('brick', 'shot')
Inputs may be any that keep to these rules, and one draw needn't show every extreme that they name: `group_size`: some shot spans all 8 bricks and some shot only 2. Window s covers model tiles window_anchor[s] to window_anchor[s] + 7. `tile_slot`: each slot of 0 to 63 once.
All inputs are finite; a program needn't handle non-finite values.
Results may differ from a plain program's by a relative error of at most 0.0003.
Values sent between devices are 32-bit elements; how exact they have to be, the bound alone decides.
No kernel may reach another device: no remote copies, remote signals or barrier semaphores. Data moves between devices by JAX's collectives and lax.ppermute only.
A program may use at most 128 MiB of HBM per device.

v0:
```python
import jax
import jax.numpy as jnp
from jax import lax
from jax.sharding import PartitionSpec as P

BLOCKS = 8
shift_beta = 0.5
relaxation = 0.8


def extended(value, sides, width):
    for axis, dim in sides:
        size, length = (lax.axis_size(axis), value.shape[dim])
        up = [(i, (i + 1) % size) for i in range(size - 1)]
        down = [(j, i) for i, j in up]
        last = lax.slice_in_dim(value, length - width, length, axis=dim)
        first = lax.slice_in_dim(value, 0, width, axis=dim)
        before = lax.ppermute(last, axis, up)
        after = lax.ppermute(first, axis, down)
        value = jnp.concatenate([before, value, after], axis=dim)
    return value


def lateral_sum(field):
    summed = jnp.zeros_like(field)
    for along_axis in (1, 3):
        widths = [(0, 0)] * 4
        widths[along_axis] = (1, 1)
        padded = jnp.pad(field, widths)
        count = field.shape[along_axis]
        summed = summed + lax.slice_in_dim(padded, 0, count, axis=along_axis)
        summed = summed + lax.slice_in_dim(padded, 2, count + 2, axis=along_axis)
    return summed


def apply_inverse(values, inv_re, inv_im):
    fwd_re = values[0] * inv_re - values[1] * inv_im
    fwd_im = values[0] * inv_im + values[1] * inv_re
    adj_re = values[2] * inv_re - values[3] * inv_im
    adj_im = values[2] * inv_im + values[3] * inv_re
    return jnp.stack([fwd_re, fwd_im, adj_re, adj_im])


def sine_taper(count, extent):
    positions = jnp.arange(count, dtype=jnp.int32).astype(jnp.float32)
    return jnp.sin(jnp.pi * (positions + 0.5) / extent)


def per_device(sources, slowness, group_size, window_anchor, tile_slot):
    slowness_window = slowness[0]
    wide_y, planes, wide_z = slowness_window.shape
    brick_index = lax.axis_index("brick")
    shot_index = lax.axis_index("shot")
    extent = group_size[shot_index] * planes
    depth_ids = brick_index * planes + jnp.arange(planes, dtype=jnp.int32)
    active = depth_ids < extent
    active_mask = active.astype(jnp.float32)[None, :, None]
    real_d = 6.0 - slowness_window
    imag_d = shift_beta * slowness_window
    denominator = real_d * real_d + imag_d * imag_d
    inv_re = real_d / denominator
    inv_im = imag_d / denominator
    forcing = sources[0].reshape(4, wide_y, planes, wide_z)
    field = relaxation * apply_inverse(forcing, inv_re, inv_im) * active_mask
    padded = extended(field, (("brick", 2),), 1)
    neighbours = padded[:, :, :-2, :] + padded[:, :, 2:, :] + lateral_sum(field)
    updated = apply_inverse(forcing + neighbours, inv_re, inv_im)
    field = ((1.0 - relaxation) * field + relaxation * updated) * active_mask
    imaging = (
        field[0] * field[2]
        - field[1] * field[3]
        - shift_beta * (field[0] * field[3] + field[1] * field[2])
    )
    extent_float = extent.astype(jnp.float32)
    depth_float = depth_ids.astype(jnp.float32)
    taper_x = jnp.where(active, jnp.sin(jnp.pi * (depth_float + 0.5) / extent_float), 0.0)
    taper_y = sine_taper(wide_y, float(wide_y))
    taper_z = sine_taper(wide_z, float(wide_z))
    gradient = imaging * (taper_y[:, None, None] * taper_x[None, :, None] * taper_z[None, None, :])
    blocks = gradient.reshape(BLOCKS, -1)
    shot_count = lax.axis_size("shot")
    tile_dev = tile_slot.shape[0] // shot_count
    owned = shot_index * tile_dev + jnp.arange(tile_dev, dtype=jnp.int32)
    piece_slots = tile_slot[window_anchor[:, None] + jnp.arange(BLOCKS, dtype=jnp.int32)[None, :]]
    weights = (owned[:, None, None] == piece_slots[None, :, :]).astype(jnp.float32)
    summed = jnp.einsum(
        "qkb,kbc->qc",
        weights,
        lax.all_gather(blocks[None], "shot", axis=0, tiled=True),
        precision=lax.Precision.HIGHEST,
    )
    return summed[None]


def solution(mesh):
    return jax.shard_map(
        per_device,
        mesh=mesh,
        in_specs=(
            P("shot", None, None, None, "brick", None),
            P("shot", None, "brick", None),
            P(),
            P(),
            P(),
        ),
        out_specs=P("brick", "shot", None),
        check_vma=False,
    )
```

profile of v0, /device:TPU:1, one launch (start us, length us, event | category | flops | bytes accessed | tf_op | source)
XLA Modules:
  0.0 342.5 jit_solution(932084848076161260)
XLA Ops:
  6.5 1.2 dynamic_slice.3
  8.4 9.2 %copy.14 = f32[1,2,2,256,8,256]{5,3,4,2,1,0:T(8,128)} copy(f32[1,2,2,256,8,256]{5,4,3,2,1,0:T(8,128)} %param.5) | data formatting | bytes 16777216 | tf_op args[0]
  17.7 5.0 %multiply_subtract_fusion.4 = (f32[1,256,8,256]{3,1,2,0:T(8,128)S(1)}, f32[1,256,8,256]{3,1,2,0:T(8,128)S(1)}, f32[1,256,8,256]{3,1,2,0:T(8,128)S(1)}, f32[1,256,8,256]{3,1,2,0:T(8,128)S(1)}) fusion(f32[4,256,8,256]{3,1,2,0:T(8,128)} %bitcast.10, f32[1,256,8,256]{3,2,1,0:T(8,128)} %param.6), kind=kLoop, calls=%fused_computation.24 | loop fusion | flops 9961472 | bytes 18874368 | tf_op jit(solution)/shard_map/sub | solution.py:37
  22.7 1.0 maximum_multiply_fusion
  23.8 0.4 copy-done.2
  24.2 0.6 copy-done.4
  24.7 0.6 copy-done.6
  25.3 3.2 copy-done.1
  28.5 1.2 fusion.15
  29.7 6.5 %collective-permute-start = (f32[4,256,1,256]{3,1,2,0:T(8,128)}, f32[4,256,1,256]{3,1,2,0:T(8,128)}, u32[]{:S(2)}, u32[]{:S(2)}) collective-permute-start(f32[4,256,1,256]{3,1,2,0:T(8,128)} %get-tuple-element.13), channel_id=1, source_target_pairs={{0,1},{1,2},{2,3},{3,4},{4,5},{5,6},{6,7},{8,9},{9,10},{10,11},{11... | collective-permute-start | bytes 3145736 | tf_op jit(solution)/shard_map/ppermute | solution.py:18
  36.2 1.3 collective-permute-start.1
  37.5 0.1 broadcast_multiply_fusion.1
  37.6 1.7 broadcast_multiply_fusion
  39.4 3.3 mul.300
  42.7 14.6 %collective-permute-done = f32[4,256,1,256]{3,1,2,0:T(8,128)} collective-permute-done((f32[4,256,1,256]{3,1,2,0:T(8,128)}, f32[4,256,1,256]{3,1,2,0:T(8,128)}, u32[]{:S(2)}, u32[]{:S(2)}) %collective-permute-start) | collective-permute-done | bytes 1048608 | tf_op jit(solution)/shard_map/ppermute | solution.py:18
  57.3 24.4 %collective-permute-done.1 = f32[4,256,1,256]{3,1,2,0:T(8,128)} collective-permute-done((f32[4,256,1,256]{3,1,2,0:T(8,128)S(1)}, f32[4,256,1,256]{3,1,2,0:T(8,128)}, u32[]{:S(2)}, u32[]{:S(2)}) %collective-permute-start.1) | collective-permute-done | bytes 1048608 | tf_op jit(solution)/shard_map/ppermute | solution.py:19
  81.8 23.0 %fusion.4 = f32[4,256,8,256]{3,1,2,0:T(8,128)S(1)} fusion(f32[4,256,8,256]{3,1,2,0:T(8,128)} %copy-done.1, f32[4,256,1,256]{3,1,2,0:T(8,128)} %collective-permute-done.1, f32[4,256,1,256]{3,1,2,0:T(8,128)} %collective-permute-done, f32[1,2,2,256,8,256]{5,3,4,2,1,0:T(8,128)} %copy.14), kind=kLoop, calls=%fused_computation.8 | loop fusion | flops 16777216 | bytes 27262976 | tf_op jit(solution)/shard_map/add | solution.py:67
  104.8 3.9 %multiply_subtract_fusion.2 = (f32[1,256,8,256]{3,1,2,0:T(8,128)S(1)}, f32[1,256,8,256]{3,1,2,0:T(8,128)}, f32[1,256,8,256]{3,1,2,0:T(8,128)}, f32[1,256,8,256]{3,1,2,0:T(8,128)}) fusion(f32[4,256,8,256]{3,1,2,0:T(8,128)S(1)} %fusion.4, f32[1,256,8,256]{3,2,1,0:T(8,128)S(1)} %copy-done.8), kind=kLoop, calls=%fused_computation.20 | loop fusion | flops 9961472 | bytes 18874368 | tf_op jit(solution)/shard_map/sub | solution.py:37
  108.8 1.1 copy-done.7
  109.9 4.2 %fusion.7 = f32[4,256,8,256]{3,1,2,0:T(8,128)S(1)} fusion(f32[1,256,8,256]{3,1,2,0:T(8,128)} %get-tuple-element.7, f32[1,256,8,256]{3,1,2,0:T(8,128)} %get-tuple-element.6, f32[1,256,8,256]{3,1,2,0:T(8,128)} %get-tuple-element.8, f32[1,256,8,256]{3,1,2,0:T(8,128)S(1)} %get-tuple-element.5, f32[8]{0:T(128)S(1)} %fusion.14, f32[8]{0:T(128)S(1)} %get-tuple-element.16, ...), kind=kLoop, calls=%fused_computation.15 | loop fusion | flops 23068672 | bytes 25165888 | tf_op jit(solution)/shard_map/mul | solution.py:68
  114.1 0.6 multiply_subtract_fusion
  114.7 2.5 copy.17
  117.2 3.4 %sub.62 = f32[1,8,65536]{2,1,0:T(8,128)} reshape(f32[1,256,8,256]{3,2,1,0:T(8,128)} %copy.17) | data formatting | bytes 4194304 | tf_op jit(solution)/shard_map/sub | solution.py:70
  120.6 3.3 mul.301
  124.0 0.6 copy-done.10
  124.6 0.1 compare_select_fusion
  124.7 0.1 reshape.222
  124.8 1.2 gather_fusion
  126.0 0.1 reshape.221
  126.1 0.1 copy.13
  126.2 172.0 %all-gather.2.cloned.1.call-done = f32[16,8,65536]{2,1,0:T(8,128)} async-done(((f32[1,8,65536]{2,1,0:T(8,128)}), f32[16,8,65536]{2,1,0:T(8,128)}) %all-gather.2.cloned.1.call-update) | async-done | bytes 33554448 | tf_op jit(solution)/shard_map/all_gather | solution.py:89
  298.1 37.6 %convolution_bitcast_fusion = f32[1,4,65536]{2,1,0:T(4,128)} fusion(f32[16,8,65536]{2,1,0:T(8,128)} %all-gather.2.cloned.1.call-done, s32[16,8]{0,1:T(8,128)S(1)} %copy.13, s32[4]{0:T(128)S(1)} %iota_add_fusion.1), kind=kOutput, calls=%fused_computation.1 | convolution fusion | flops 402653696 | bytes 34603536 | tf_op jit(solution)/shard_map/qkb,kbc->qc/dot_general | solution.py:86
  (23 shorter events, 0.2 us)
Async XLA Ops:
  6.5 118.2 %copy-start = (s32[64]{0:T(128)S(1)}, s32[64]{0:T(128)}, u32[]{:S(2)}) copy-start(s32[64]{0:T(128)} %param.9) | copy-start | bytes 772
  6.5 291.6 %all-gather.2.cloned.1.call-start = ((), (), s32[]{:S(2)}) async-start(), calls=%async_computation | async-start | bytes 35651584 | tf_op jit(solution)/shard_map/all_gather | solution.py:89
  22.7 1.5 copy-start.2
  22.7 2.0 copy-start.4
  22.7 2.6 copy-start.6
  25.3 3.2 copy-start.1
  29.7 27.6 %collective-permute-start = (f32[4,256,1,256]{3,1,2,0:T(8,128)}, f32[4,256,1,256]{3,1,2,0:T(8,128)}, u32[]{:S(2)}, u32[]{:S(2)}) collective-permute-start(f32[4,256,1,256]{3,1,2,0:T(8,128)} %get-tuple-element.13), channel_id=1, source_target_pairs={{0,1},{1,2},{2,3},{3,4},{4,5},{5,6},{6,7},{8,9},{9,10},{10,11},{11... | collective-permute-start | bytes 3145736 | tf_op jit(solution)/shard_map/ppermute | solution.py:18
  36.2 45.6 %collective-permute-start.1 = (f32[4,256,1,256]{3,1,2,0:T(8,128)S(1)}, f32[4,256,1,256]{3,1,2,0:T(8,128)}, u32[]{:S(2)}, u32[]{:S(2)}) collective-permute-start(f32[4,256,1,256]{3,1,2,0:T(8,128)S(1)} %get-tuple-element.14), channel_id=1, source_target_pairs={{1,0},{2,1},{3,2},{4,3},{5,4},{6,5},{7,6},{9,8},{10,9},{11,10},{12... | collective-permute-start | bytes 3145736 | tf_op jit(solution)/shard_map/ppermute | solution.py:19
  42.7 62.1 %copy-start.8 = (f32[1,256,8,256]{3,2,1,0:T(8,128)S(1)}, f32[1,256,8,256]{3,2,1,0:T(8,128)}, u32[]{:S(2)}) copy-start(f32[1,256,8,256]{3,2,1,0:T(8,128)} %param.6) | copy-start | bytes 6291460
  104.8 4.0 %copy-start.3 = (f32[1,256,8,256]{3,1,2,0:T(8,128)S(1)}, f32[1,256,8,256]{3,1,2,0:T(8,128)}, u32[]{:S(2)}) copy-start(f32[1,256,8,256]{3,1,2,0:T(8,128)} %copy-done.2) | copy-start | bytes 6291460
  104.8 4.0 %copy-start.5 = (f32[1,256,8,256]{3,1,2,0:T(8,128)S(1)}, f32[1,256,8,256]{3,1,2,0:T(8,128)}, u32[]{:S(2)}) copy-start(f32[1,256,8,256]{3,1,2,0:T(8,128)} %copy-done.4) | copy-start | bytes 6291460
  104.8 5.1 %copy-start.7 = (f32[1,256,8,256]{3,1,2,0:T(8,128)S(1)}, f32[1,256,8,256]{3,1,2,0:T(8,128)}, u32[]{:S(2)}) copy-start(f32[1,256,8,256]{3,1,2,0:T(8,128)} %copy-done.6) | copy-start | bytes 6291460
  117.2 3.4 %copy-start.9 = (f32[1,8,65536]{2,1,0:T(8,128)S(1)}, f32[1,8,65536]{2,1,0:T(8,128)}, u32[]{:S(2)}) copy-start(f32[1,8,65536]{2,1,0:T(8,128)} %mul.300) | copy-start | bytes 6291460
  123.9 0.7 copy-start.10
Sparse Core Ops, SparseCore 0:
  124.1 174.0 all-gather.1
where the time goes:
time: 343 us
  waiting for transfers between devices  211 us (62%)
  other arithmetic  43.1 us (13%)
  matrix products  37.6 us (11%)
  local copies, waits for them, and re-layouts  28.9 us (8%)
  between operations  14.2 us (4%)
  starting transfers between devices  7.77 us (2%)
    all_gather x1, waiting for transfers between devices, per_device(): lax.all_gather(blocks[None], 'shot', axis=0, tiled=True)  172 us
    dot_general x1, matrix products, per_device(): jnp.einsum('qkb,kbc->qc', weights, lax.all_gather(blocks[None], 'shot', a...  37.6 us
    ppermute x1, waiting for transfers between devices, extended(): after = lax.ppermute(first, axis, down)  24.4 us
    add x1, other arithmetic, per_device(): updated = apply_inverse(forcing + neighbours, inv_re, inv_im)  23 us
    unnamed x23, local copies, waits for them, and re-layouts  15.7 us
    ppermute x1, waiting for transfers between devices, extended(): before = lax.ppermute(last, axis, up)  14.6 us
    sub x2, other arithmetic, apply_inverse(): fwd_re = values[0] * inv_re - values[1] * inv_im  8.95 us
  transfers between devices with their start and end apart: 3, of which 3 were waited for; matrix products, arithmetic and copies ran while one was open for 2% of the time, Pallas kernels for 0%

commit v1 on v0

--- a/solution.py
+++ b/solution.py
@@ -86,7 +86,9 @@
     summed = jnp.einsum(
         "qkb,kbc->qc",
         weights,
-        lax.all_gather(blocks[None], "shot", axis=0, tiled=True),
+        jnp.concatenate(
+            lax.all_to_all(jnp.stack([blocks[None]] * lax.axis_size("shot")), "shot", 0, 0), axis=0
+        ),
         precision=lax.Precision.HIGHEST,
     )
     return summed[None]

time: 343 us -> 537 us (1.57)
  waiting for transfers between devices: 211 us -> 401 us
  between operations: 14.2 us -> 0.81 us
  local copies, waits for them, and re-layouts: 28.9 us -> 39.5 us
  starting transfers between devices: 7.77 us -> 15.7 us
    all_to_all x0 -> x1, waiting for transfers between devices: none -> 362 us  [per_device(): lax.all_to_all(jnp.stack([blocks[None]] * lax.axis_size('shot')), 'shot',...]
    all_gather x1 -> x0, waiting for transfers between devices: 172 us -> none  [per_device(): lax.all_gather(blocks[None], 'shot', axis=0, tiled=True)]
    another operation x0 -> x1, local copies, waits for them, and re-layouts: none -> 11.2 us  [per_device(): jnp.stack([blocks[None]] * lax.axis_size('shot'))]
    all_to_all x0 -> x1, starting transfers between devices: none -> 7.93 us  [per_device(): lax.all_to_all(jnp.stack([blocks[None]] * lax.axis_size('shot')), 'shot',...]
  transfers between devices with their start and end apart: 3 -> 3, of which waited for: 3 -> 3; matrix products, arithmetic and copies ran while one was open for 2% -> 1% of each run, Pallas kernels for 0% -> 0%
where the time goes in v1:
time: 537 us
  waiting for transfers between devices  401 us (75%)
  other arithmetic  41.9 us (8%)
  local copies, waits for them, and re-layouts  39.5 us (7%)
  matrix products  37.6 us (7%)
  starting transfers between devices  15.7 us (3%)
    all_to_all x1, waiting for transfers between devices, per_device(): lax.all_to_all(jnp.stack([blocks[None]] * lax.axis_size('shot')), 'shot',...  362 us
    dot_general x1, matrix products, per_device(): jnp.einsum('qkb,kbc->qc', weights, jnp.concatenate(lax.all_to_all(jnp.sta...  37.6 us
    ppermute x1, waiting for transfers between devices, extended(): after = lax.ppermute(first, axis, down)  24.4 us
    add x1, other arithmetic, per_device(): updated = apply_inverse(forcing + neighbours, inv_re, inv_im)  23.1 us
    unnamed x23, local copies, waits for them, and re-layouts  15.1 us
    ppermute x1, waiting for transfers between devices, extended(): before = lax.ppermute(last, axis, up)  14.6 us
    another operation x1, local copies, waits for them, and re-layouts, per_device(): jnp.stack([blocks[None]] * lax.axis_size('shot'))  11.2 us
  transfers between devices with their start and end apart: 3, of which 3 were waited for; matrix products, arithmetic and copies ran while one was open for 1% of the time, Pallas kernels for 0%

profile of v1, /device:TPU:1, one launch (start us, length us, event | category | flops | bytes accessed | tf_op | source)
XLA Modules:
  0.0 536.7 jit_solution(379272933272852218)
XLA Ops:
  0.0 1.2 dynamic_slice.3
  1.9 9.2 %copy.14 = f32[1,2,2,256,8,256]{5,3,4,2,1,0:T(8,128)} copy(f32[1,2,2,256,8,256]{5,4,3,2,1,0:T(8,128)} %param.5) | data formatting | bytes 16777216 | tf_op args[0]
  11.1 5.0 multiply_subtract_fusion.4
  16.2 1.0 maximum_multiply_fusion
  17.2 0.4 copy-done.2
  17.6 0.6 copy-done.4
  18.2 0.6 copy-done.6
  18.8 3.2 copy-done.1
  22.0 1.2 fusion.16
  23.2 6.5 %collective-permute-start = (f32[4,256,1,256]{3,1,2,0:T(8,128)}, f32[4,256,1,256]{3,1,2,0:T(8,128)}, u32[]{:S(2)}, u32[]{:S(2)}) collective-permute-start(f32[4,256,1,256]{3,1,2,0:T(8,128)} %get-tuple-element.13), channel_id=1, source_target_pairs={{0,1},{1,2},{2,3},{3,4},{4,5},{5,6},{6,7},{8,9},{9,10},{10,11},{11... | collective-permute-start | bytes 3145736 | tf_op jit(solution)/shard_map/ppermute | solution.py:18
  29.7 1.3 collective-permute-start.1
  31.0 0.1 broadcast_multiply_fusion.1
  31.1 1.7 broadcast_multiply_fusion
  32.8 3.3 mul.286
  36.1 14.6 %collective-permute-done = f32[4,256,1,256]{3,1,2,0:T(8,128)} collective-permute-done((f32[4,256,1,256]{3,1,2,0:T(8,128)}, f32[4,256,1,256]{3,1,2,0:T(8,128)}, u32[]{:S(2)}, u32[]{:S(2)}) %collective-permute-start) | collective-permute-done | bytes 1048608 | tf_op jit(solution)/shard_map/ppermute | solution.py:18
  50.8 24.4 %collective-permute-done.1 = f32[4,256,1,256]{3,1,2,0:T(8,128)} collective-permute-done((f32[4,256,1,256]{3,1,2,0:T(8,128)S(1)}, f32[4,256,1,256]{3,1,2,0:T(8,128)}, u32[]{:S(2)}, u32[]{:S(2)}) %collective-permute-start.1) | collective-permute-done | bytes 1048608 | tf_op jit(solution)/shard_map/ppermute | solution.py:19
  75.2 23.1 %fusion.5 = f32[4,256,8,256]{3,1,2,0:T(8,128)S(1)} fusion(f32[4,256,8,256]{3,1,2,0:T(8,128)} %copy-done.1, f32[4,256,1,256]{3,1,2,0:T(8,128)} %collective-permute-done.1, f32[4,256,1,256]{3,1,2,0:T(8,128)} %collective-permute-done, f32[1,2,2,256,8,256]{5,3,4,2,1,0:T(8,128)} %copy.14), kind=kLoop, calls=%fused_computation.9 | loop fusion | flops 16777216 | bytes 27262976 | tf_op jit(solution)/shard_map/add | solution.py:67
  98.4 3.9 multiply_subtract_fusion.2
  102.4 1.1 copy-done.7
  103.5 4.2 fusion.8
  107.7 0.6 multiply_subtract_fusion
  108.3 2.5 copy.17
  110.8 3.5 sub.58
  114.3 2.0 mul.287
  116.2 11.2 %stack.8 = f32[16,1,8,65536]{3,2,1,0:T(8,128)} broadcast(f32[8,65536]{1,0:T(8,128)S(1)} %mul.287), dimensions={2,3} | broadcast | bytes 35651584 | tf_op jit(solution)/shard_map/stack | solution.py:90
  127.5 7.9 %all-to-all-start = ((f32[16,1,8,65536]{3,2,1,0:T(8,128)}), f32[16,1,8,65536]{3,2,1,0:T(8,128)}, u32[]{:S(2)}, u32[]{:S(2)}) async-start(f32[16,1,8,65536]{3,2,1,0:T(8,128)} %stack.8), calls=%async_computation | async-start | bytes 67108864 | tf_op jit(solution)/shard_map/all_to_all | solution.py:90
  135.4 0.1 compare_select_fusion
  135.5 0.1 reshape.182
  135.6 1.2 gather_fusion
  136.8 0.1 reshape.181
  137.0 362.2 %all-to-all-done = f32[16,1,8,65536]{3,2,1,0:T(8,128)} async-done(((f32[16,1,8,65536]{3,2,1,0:T(8,128)}), f32[16,1,8,65536]{3,2,1,0:T(8,128)}, u32[]{:S(2)}, u32[]{:S(2)}) %all-to-all-start) | async-done | bytes 33554464 | tf_op jit(solution)/shard_map/all_to_all | solution.py:90
  499.2 37.6 %convolution_bitcast_fusion = f32[1,4,65536]{2,1,0:T(4,128)} fusion(f32[16,1,8,65536]{3,2,1,0:T(8,128)} %all-to-all-done, s32[16,8]{0,1:T(8,128)S(1)} %copy.13, s32[4]{0:T(128)S(1)} %iota_add_fusion.1), kind=kOutput, calls=%fused_computation.1 | convolution fusion | flops 402653696 | bytes 34603536 | tf_op jit(solution)/shard_map/qkb,kbc->qc/dot_general | solution.py:86
  (23 shorter events, 0.2 us)
Async XLA Ops:
  0.0 135.6 %copy-start = (s32[64]{0:T(128)S(1)}, s32[64]{0:T(128)}, u32[]{:S(2)}) copy-start(s32[64]{0:T(128)} %param.9) | copy-start | bytes 772
  16.2 1.5 copy-start.2
  16.2 2.0 copy-start.4
  16.2 2.6 copy-start.6
  18.8 3.2 copy-start.1
  23.2 27.6 %collective-permute-start = (f32[4,256,1,256]{3,1,2,0:T(8,128)}, f32[4,256,1,256]{3,1,2,0:T(8,128)}, u32[]{:S(2)}, u32[]{:S(2)}) collective-permute-start(f32[4,256,1,256]{3,1,2,0:T(8,128)} %get-tuple-element.13), channel_id=1, source_target_pairs={{0,1},{1,2},{2,3},{3,4},{4,5},{5,6},{6,7},{8,9},{9,10},{10,11},{11... | collective-permute-start | bytes 3145736 | tf_op jit(solution)/shard_map/ppermute | solution.py:18
  29.7 45.6 %collective-permute-start.1 = (f32[4,256,1,256]{3,1,2,0:T(8,128)S(1)}, f32[4,256,1,256]{3,1,2,0:T(8,128)}, u32[]{:S(2)}, u32[]{:S(2)}) collective-permute-start(f32[4,256,1,256]{3,1,2,0:T(8,128)S(1)} %get-tuple-element.14), channel_id=1, source_target_pairs={{1,0},{2,1},{3,2},{4,3},{5,4},{6,5},{7,6},{9,8},{10,9},{11,10},{12... | collective-permute-start | bytes 3145736 | tf_op jit(solution)/shard_map/ppermute | solution.py:19
  36.1 62.3 %copy-start.8 = (f32[1,256,8,256]{3,2,1,0:T(8,128)S(1)}, f32[1,256,8,256]{3,2,1,0:T(8,128)}, u32[]{:S(2)}) copy-start(f32[1,256,8,256]{3,2,1,0:T(8,128)} %param.6) | copy-start | bytes 6291460
  98.4 4.0 copy-start.3
  98.4 4.0 copy-start.5
  98.4 5.1 copy-start.7
  110.8 3.5 copy-start.9
  127.5 7.9 %copy-start.10 = (s32[16]{0:T(128)S(1)}, s32[16]{0:T(128)}, u32[]{:S(2)}) copy-start(s32[16]{0:T(128)} %param.8) | copy-start | bytes 196
  127.5 371.7 %all-to-all-start = ((f32[16,1,8,65536]{3,2,1,0:T(8,128)}), f32[16,1,8,65536]{3,2,1,0:T(8,128)}, u32[]{:S(2)}, u32[]{:S(2)}) async-start(f32[16,1,8,65536]{3,2,1,0:T(8,128)} %stack.8), calls=%async_computation | async-start | bytes 67108864 | tf_op jit(solution)/shard_map/all_to_all | solution.py:90
